TPU v7x, 32 devices: a whole 2x2x4 slice. The times are simulated.
32 devices in a mesh: groups: 2 (over y), tensor: 4 (over z), seq: 2 (over x), load: 2 (over core).
Axes of the slice: x: 2, y: 2, z: 4, core: 2. Of those that a mesh axis runs over, the one named last changes fastest.
Arguments:
- tokens: bfloat16 [1024, 16384], P(('groups', 'tensor'), ('seq', 'load')), parts along dimension 0, may hold values from -21 to 21
- weight_query: bfloat16 [16384, 16384], P(('seq', 'load'), 'tensor'), may hold values from -0.046875 to 0.046875
- weight_keyval: bfloat16 [16384, 2048], P(('seq', 'load'), 'tensor'), may hold values from -0.046875 to 0.046875
- down_query: bfloat16 [16384, 1024], P(('seq', 'load'), ('groups', 'tensor')), parts along dimension 1, may hold values from -0.046875 to 0.046875
- down_keyval: bfloat16 [16384, 1024], P(('seq', 'load'), ('groups', 'tensor')), parts along dimension 1, may hold values from -0.046875 to 0.046875
- up_query: bfloat16 [1024, 16384], P(('groups', 'load'), 'tensor'), parts along dimension 0, may hold values from -0.5 to 0.5
- up_keyval: bfloat16 [1024, 2048], P(('groups', 'load'), 'tensor'), parts along dimension 0, may hold values from -0.5 to 0.5
- adapter_rank: int32 [8], P('groups'), parts along dimension 0, may hold values from 8 to 128, as said below
- token_lengths: int32 [8], P('groups'), parts along dimension 0, may hold values from 1 to 384, 512 in all
- adapter_slot: int32 [8], P('groups'), parts along dimension 0, may hold values from 0 to 3, each once
Outputs:
- context: bfloat16 [1024, 16384], P(('groups', 'seq', 'load'), 'tensor'), parts along dimension 0
- kv_cache: bfloat16 [1024, 2048], P(('groups', 'seq', 'load'), 'tensor'), parts along dimension 0
There are 2 independent parts, one for each index of `groups`. A program takes and returns all parts, laid end to end along the dimension named above; an argument that names none is the same for every part. Nothing has to cross between parts.
Inputs may be any that keep to these rules, and one draw needn't show every extreme that they name: `adapter_rank`: each rank is a power of two; some tenant has rank 128 and some has rank 8. `token_lengths`: the lengths sum to 512; some tenant has exactly 384 tokens. `adapter_slot`: each slot belongs to exactly one tenant.
All inputs are finite; a program needn't handle non-finite values.
Results may differ from a plain program's by a relative error of at most 0.0025.
The roundings to bfloat16 on the way count: a program that leaves them out, or rounds other values in their place, can miss the bound.
Values may be sent and summed in bfloat16 or wider, within the bound.
No kernel may reach another device: no remote copies, remote signals or barrier semaphores. Data moves between devices by JAX's collectives and lax.ppermute only.
A program may use at most 128 MiB of HBM per device.

v0:
```python
import math
import jax
import jax.numpy as jnp
from jax import lax
from jax.sharding import PartitionSpec as P

HEADS = 128
KV_HEADS = 8
HEAD_DIM = 128
TENANTS = 4
ROPE_BASE = 500000.0
ADAPTER_ALPHA = 8.0


def product(left, right):
    return jnp.dot(left, right, preferred_element_type=jnp.float32)


def rotate_pairs(values, position, first_col):
    pair_count = values.shape[1] // 2
    pair_col = first_col + 2 * jnp.arange(pair_count, dtype=jnp.int32)
    within = pair_col % HEAD_DIM // 2
    frequency = jnp.exp(-(2.0 * within.astype(jnp.float32) / HEAD_DIM) * math.log(ROPE_BASE))
    angles = position.astype(jnp.float32)[:, None] * frequency[None, :]
    pair_view = values.reshape(values.shape[0], pair_count, 2)
    even_part = pair_view[:, :, 0]
    odd_part = pair_view[:, :, 1]
    cosine = jnp.cos(angles)
    sine_angle = jnp.sin(angles)
    turned = jnp.stack(
        [even_part * cosine - odd_part * sine_angle, even_part * sine_angle + odd_part * cosine],
        axis=2,
    )
    return turned.reshape(values.shape)


def tenant_table(token_ids, adapter_rank, token_lengths, adapter_slot):
    segment_ends = jnp.cumsum(token_lengths)
    begins = segment_ends - token_lengths
    owned_rows = (token_ids[:, None] >= begins[None, :]) & (
        token_ids[:, None] < segment_ends[None, :]
    )
    zero_int = jnp.zeros((), jnp.int32)
    own_rank = jnp.sum(jnp.where(owned_rows, adapter_rank[None, :], zero_int), axis=1)
    own_slot = jnp.sum(jnp.where(owned_rows, adapter_slot[None, :], zero_int), axis=1)
    own_first = jnp.sum(jnp.where(owned_rows, begins[None, :], zero_int), axis=1)
    slot_hot = own_slot[:, None] == jnp.arange(TENANTS, dtype=jnp.int32)[None, :]
    return (own_rank, own_first, slot_hot)


def select_slot(down_values, slot_hot):
    shaped = down_values.reshape(down_values.shape[0], -1, TENANTS)
    return jnp.sum(jnp.where(slot_hot[:, None, :], shaped, 0.0), axis=2)


def scale_ranks(picked, own_rank, first_rank):
    rank_index = first_rank + jnp.arange(picked.shape[1], dtype=jnp.int32)
    keep_mask = rank_index[None, :] < own_rank[:, None]
    factor = ADAPTER_ALPHA / jnp.sqrt(own_rank.astype(jnp.float32))
    return jnp.where(keep_mask, picked * factor[:, None], 0.0).astype(jnp.bfloat16)


def widen_slots(low_values, slot_hot):
    wide_rows = jnp.where(
        slot_hot[:, None, :], low_values[:, :, None], jnp.zeros((), low_values.dtype)
    )
    return wide_rows.reshape(low_values.shape[0], -1)


def shards(
    tokens,
    weight_query,
    weight_keyval,
    down_query,
    down_keyval,
    up_query,
    up_keyval,
    adapter_rank,
    token_lengths,
    adapter_slot,
):
    tensor_count = lax.axis_size("tensor")
    block_count = lax.axis_size(("seq", "load"))
    tensor_index = lax.axis_index("tensor")
    block_index = lax.axis_index(("seq", "load"))
    query_cols = weight_query.shape[1]
    keyval_cols = weight_keyval.shape[1]
    rank_share = down_query.shape[1] // TENANTS
    block_rows = tokens.shape[0] * tensor_count // block_count
    shard_rows = lax.all_gather(tokens, "tensor", axis=0, tiled=True)
    piece_ids = jnp.arange(shard_rows.shape[0], dtype=jnp.int32)
    piece_rank, piece_first, piece_hot = tenant_table(
        piece_ids, adapter_rank, token_lengths, adapter_slot
    )
    columns_list = [
        product(shard_rows, weight_query),
        product(shard_rows, weight_keyval),
        select_slot(product(shard_rows, down_query), piece_hot),
        select_slot(product(shard_rows, down_keyval), piece_hot),
    ]
    partial_terms = jnp.concatenate(columns_list, axis=1)
    summed = lax.psum_scatter(partial_terms, ("seq", "load"), scatter_dimension=0, tiled=True)
    token_ids = block_index * block_rows + jnp.arange(block_rows, dtype=jnp.int32)
    own_rank, own_first, slot_hot = tenant_table(
        token_ids, adapter_rank, token_lengths, adapter_slot
    )
    position = token_ids - own_first
    low_start = query_cols + keyval_cols
    first_rank = tensor_index * rank_share
    low_query = scale_ranks(summed[:, low_start : low_start + rank_share], own_rank, first_rank)
    low_keyval = scale_ranks(summed[:, low_start + rank_share :], own_rank, first_rank)
    full_query, full_keyval = (
        lax.all_gather(low_query, "tensor", axis=1, tiled=True),
        lax.all_gather(low_keyval, "tensor", axis=1, tiled=True),
    )
    wide_query = widen_slots(full_query, slot_hot)
    wide_keyval = widen_slots(full_keyval, slot_hot)
    up_query_all, up_keyval_all = (
        lax.all_gather(up_query, "load", axis=0, tiled=True),
        lax.all_gather(up_keyval, "load", axis=0, tiled=True),
    )
    delta_query = product(wide_query, up_query_all)
    delta_keyval = product(wide_keyval, up_keyval_all)
    query_rows = rotate_pairs(
        summed[:, :query_cols] + delta_query, position, tensor_index * query_cols
    ).astype(jnp.bfloat16)
    keyval = summed[:, query_cols:low_start] + delta_keyval
    kv_first_col = tensor_index * keyval_cols
    is_key = kv_first_col + jnp.arange(keyval_cols, dtype=jnp.int32) < KV_HEADS * HEAD_DIM
    kv_local = jnp.where(
        is_key[None, :], rotate_pairs(keyval, position, kv_first_col), keyval
    ).astype(jnp.bfloat16)
    kv_all = lax.all_gather(kv_local, "tensor", axis=1, tiled=True)
    heads_here = query_cols // HEAD_DIM
    group_size = HEADS // KV_HEADS
    kv_here = max(heads_here // group_size, 1)
    per_kv = heads_here // kv_here
    kv_first = tensor_index * heads_here // group_size
    key_cols = KV_HEADS * HEAD_DIM
    key_heads = lax.dynamic_slice_in_dim(
        kv_all, kv_first * HEAD_DIM, kv_here * HEAD_DIM, 1
    ).reshape(block_rows, kv_here, HEAD_DIM)
    value_heads = lax.dynamic_slice_in_dim(
        kv_all, key_cols + kv_first * HEAD_DIM, kv_here * HEAD_DIM, 1
    ).reshape(block_rows, kv_here, HEAD_DIM)
    grouped = query_rows.reshape(block_rows, kv_here, per_kv, HEAD_DIM)
    running_top = jnp.full((kv_here, per_kv, block_rows), -1e30, jnp.float32)
    piece_keys = lax.all_gather(key_heads, ("seq", "load"), axis=0, tiled=True)
    piece_values = lax.all_gather(value_heads, ("seq", "load"), axis=0, tiled=True)
    key_ids = jnp.arange(piece_keys.shape[0], dtype=jnp.int32)
    visible = (key_ids[None, :] >= own_first[:, None]) & (key_ids[None, :] <= token_ids[:, None])
    scores = jnp.einsum(
        "qghd,kgd->ghqk", grouped, piece_keys, preferred_element_type=jnp.float32
    ) / math.sqrt(HEAD_DIM)
    scores = jnp.where(visible, scores, -1e30)
    new_top = jnp.maximum(running_top, jnp.max(scores, axis=3))
    exp_scores = jnp.where(visible, jnp.exp(scores - new_top[..., None]), 0.0)
    new_sum = jnp.sum(exp_scores, axis=3)
    new_acc = jnp.einsum(
        "ghqk,kgd->ghqd",
        exp_scores.astype(jnp.bfloat16),
        piece_values,
        preferred_element_type=jnp.float32,
    )
    state_tuple = (new_top, new_sum, new_acc)
    final_top, row_total, accumulated = state_tuple
    context = (accumulated / row_total[..., None]).astype(jnp.bfloat16)
    context = jnp.transpose(context, (2, 0, 1, 3)).reshape(block_rows, query_cols)
    return (context, kv_local)


def solution(mesh):
    placed = (
        P(("groups", "tensor"), ("seq", "load")),
        P(("seq", "load"), "tensor"),
        P(("seq", "load"), "tensor"),
        P(("seq", "load"), ("groups", "tensor")),
        P(("seq", "load"), ("groups", "tensor")),
        P(("groups", "load"), "tensor"),
        P(("groups", "load"), "tensor"),
        P("groups"),
        P("groups"),
        P("groups"),
    )
    return jax.shard_map(
        shards,
        mesh=mesh,
        in_specs=placed,
        out_specs=(P(("groups", "seq", "load"), "tensor"), P(("groups", "seq", "load"), "tensor")),
        check_vma=False,
    )
```

profile of v0, /device:TPU:0, one launch (start us, length us, event | category | flops | bytes accessed | tf_op | source)
XLA Modules:
  0.0 307.8 jit_solution(12603682997678167109)
XLA Ops:
  8.0 0.0 copy-start
  8.0 0.0 copy-start.4
  8.0 0.0 all-gather.3.cloned.1.call-start
  8.1 0.7 all-gather.3.cloned.1.call-update
  8.8 0.0 reduce-scatter.2.cloned.1.call-start
  8.8 0.8 reduce-window.8
  9.6 0.7 bitcast_subtract_fusion
  10.3 0.7 select_reduce_fusion.2
  11.0 82.9 %all-gather.3.cloned.1.call-done = bf16[512,4096]{1,0:T(8,128)(2,1)} async-done(((bf16[128,4096]{1,0:T(8,128)(2,1)}), bf16[512,4096]{1,0:T(8,128)(2,1)}) %all-gather.3.cloned.1.call-update) | async-done | bytes 4194320 | tf_op jit(solution)/shard_map/all_gather | solution.py:90
  93.9 0.0 copy-done
  93.9 3.7 %fusion.46 = f32[512,128]{0,1:T(8,128)S(1)} fusion(bf16[512,4096]{1,0:T(8,128)(2,1)} %all-gather.3.cloned.1.call-done, bf16[4096,128]{1,0:T(8,128)(2,1)S(1)} %copy-done), kind=kOutput, calls=%fused_computation.100 | convolution fusion | flops 536870912 | bytes 5505024 | tf_op jit(solution)/shard_map/dot_general | solution.py:16
  97.6 0.1 reshape.386
  97.7 0.0 copy-done.4
  97.7 3.7 %fusion.47 = f32[512,128]{0,1:T(8,128)S(1)} fusion(bf16[512,4096]{1,0:T(8,128)(2,1)} %all-gather.3.cloned.1.call-done, bf16[4096,128]{1,0:T(8,128)(2,1)S(1)} %copy-done.4), kind=kOutput, calls=%fused_computation.101 | convolution fusion | flops 536870912 | bytes 5505024 | tf_op jit(solution)/shard_map/dot_general | solution.py:16
  101.4 0.1 reshape.387
  101.5 0.3 select_reduce_fusion.1
  101.9 0.0 copy-start.2
  101.9 26.5 %fusion.44 = f32[512,4096]{0,1:T(8,128)} fusion(bf16[512,4096]{1,0:T(8,128)(2,1)} %all-gather.3.cloned.1.call-done, bf16[4096,4096]{1,0:T(8,128)(2,1)} %param.11), kind=kOutput, calls=%fused_computation.98 | convolution fusion | flops 17179869184 | bytes 46137344 | tf_op jit(solution)/shard_map/dot_general | solution.py:16
  128.4 0.0 copy-done.2
  128.4 0.0 copy-start.3
  128.4 4.7 %fusion.45 = f32[512,512]{0,1:T(8,128)S(1)} fusion(bf16[512,4096]{1,0:T(8,128)(2,1)S(1)} %copy-done.2, bf16[4096,512]{1,0:T(8,128)(2,1)} %param.12), kind=kOutput, calls=%fused_computation.99 | convolution fusion | flops 2147483648 | bytes 9437184 | tf_op jit(solution)/shard_map/dot_general | solution.py:16
  133.1 0.0 copy-done.3
  133.1 9.8 %pad_maximum_fusion = f32[512,4672]{0,1:T(8,128)} fusion(f32[512,32]{0,1:T(8,128)S(1)} %get-tuple-element.13, f32[512,32]{0,1:T(8,128)S(1)} %get-tuple-element.12, f32[512,512]{0,1:T(8,128)S(1)} %fusion.45, f32[512,4096]{0,1:T(8,128)S(1)} %copy-done.3), kind=kLoop, calls=%fused_computation | loop fusion | flops 7176192 | bytes 19136512 | tf_op jit(solution)/shard_map/concatenate | solution.py:101
  142.9 0.0 copy-start.6
  142.9 0.0 copy-start.7
  142.9 0.0 reduce-scatter.2.cloned.1.call-update
  142.9 0.0 all-gather.5.cloned.1.call-start
  142.9 0.5 all-gather.5.cloned.1.call-update
  143.6 0.0 copy-done.6
  143.6 0.0 copy-done.7
  143.6 0.1 select_reduce_fusion.5
  143.7 0.1 copy-done.5
  143.8 2.2 all_gather.26
  146.0 0.1 fusion.20
  146.1 76.7 %reduce-scatter.2.cloned.1.call-done = f32[128,4672]{0,1:T(8,128)} async-done(((f32[512,4672]{0,1:T(8,128)}), f32[128,4672]{0,1:T(8,128)}) %reduce-scatter.2.cloned.1.call-update) | async-done | bytes 2392080 | tf_op jit(solution)/shard_map/reduce_scatter | solution.py:102
  222.8 0.8 fusion.27
  223.7 13.2 %all_gather.25 = bf16[128,128]{0,1:T(8,128)(2,1)S(1)} all-gather(bf16[128,32]{0,1:T(8,128)(2,1)S(1)} %get-tuple-element.17), channel_id=1, replica_groups=mesh['groups'=2,'tensor'=4,'seq'=2,'load'=2] {'tensor'}, dimensions={1}, use_global_device_ids=true | all-gather | bytes 40960 | tf_op jit(solution)/shard_map/all_gather | solution.py:114
  236.8 13.1 %all_gather.29 = bf16[128,128]{0,1:T(8,128)(2,1)S(1)} all-gather(bf16[128,32]{0,1:T(8,128)(2,1)S(1)} %get-tuple-element.18), channel_id=1, replica_groups=mesh['groups'=2,'tensor'=4,'seq'=2,'load'=2] {'tensor'}, dimensions={1}, use_global_device_ids=true | all-gather | bytes 40960 | tf_op jit(solution)/shard_map/all_gather | solution.py:113
  250.0 0.1 broadcast_select_fusion.1
  250.1 1.3 convolution_add_fusion.1
  251.4 0.2 fusion.43
  251.6 0.1 copy.76
  251.7 0.1 copy.77
  251.8 0.6 fusion.25
  252.4 0.1 copy.59
  252.5 0.1 select_convert_fusion
  252.7 0.8 copy.68
  253.4 15.4 %all_gather.27 = bf16[128,2048]{0,1:T(8,128)(2,1)S(1)} all-gather(bf16[128,512]{0,1:T(8,128)(2,1)S(1)} %select_convert_fusion), channel_id=1, replica_groups=mesh['groups'=2,'tensor'=4,'seq'=2,'load'=2] {'tensor'}, dimensions={1}, use_global_device_ids=true | all-gather | bytes 655360 | tf_op jit(solution)/shard_map/all_gather | solution.py:133
  268.9 0.1 copy.60
  269.0 5.8 %all_gather.28 = bf16[512,2,128]{2,0,1:T(8,128)(2,1)S(1)} all-gather(bf16[128,2,128]{2,0,1:T(8,128)(2,1)S(1)} %copy.60), channel_id=1, replica_groups=mesh['groups'=2,'tensor'=4,'seq'=2,'load'=2] {'seq','load'}, dimensions={0}, use_global_device_ids=true | all-gather | bytes 327680 | tf_op jit(solution)/shard_map/all_gather | solution.py:148
  274.8 4.6 %convolution_add_fusion = f32[128,4096]{0,1:T(8,128)S(1)} fusion(bf16[128,512]{0,1:T(8,128)(2,1)S(1)} %bitcast.63, bf16[512,4096]{1,0:T(8,128)(2,1)} %all-gather.5.cloned.1.call-done, f32[128,4672]{0,1:T(8,128)} %reduce-scatter.2.cloned.1.call-done), kind=kOutput, calls=%fused_computation.6 | convolution fusion | flops 537395200 | bytes 8519680 | tf_op jit(solution)/shard_map/dot_general | solution.py:16
  279.4 1.7 fusion.42
  281.1 0.7 copy.78
  281.7 0.7 copy.79
  282.4 4.2 %fusion.14 = (bf16[128,2048,1]{1,0,2:T(8,128)(2,1)S(1)}, bf16[128,2048,1]{1,0,2:T(8,128)(2,1)S(1)}) fusion(f32[128,2048,1]{1,0,2:T(8,128)S(1)} %copy.79, f32[128,2048,1]{1,0,2:T(8,128)S(1)} %copy.78, f32[2048]{0:T(1024)S(1)} %fusion.35, f32[128]{0:T(128)S(1)} %subtract_convert_fusion), kind=kLoop, calls=%fused_computation.19 | loop fusion | flops 2359296 | bytes 3154432 | tf_op jit(solution)/shard_map/convert
  286.6 0.1 pad_maximum_fusion.1
  286.7 0.8 copy.64
  287.5 1.3 fusion
  288.8 5.9 %all_gather.31 = bf16[512,2,128]{0,2,1:T(8,128)(2,1)S(1)} all-gather(bf16[128,2,128]{0,2,1:T(8,128)(2,1)S(1)} %bitcast.66), channel_id=1, replica_groups=mesh['groups'=2,'tensor'=4,'seq'=2,'load'=2] {'seq','load'}, dimensions={0}, use_global_device_ids=true | all-gather | bytes 327680 | tf_op jit(solution)/shard_map/all_gather | solution.py:149
  294.7 2.0 fusion.1
  296.8 0.0 copy-start.1
  296.8 2.2 fusion.6
  299.0 1.3 copy.67
  300.3 0.0 copy-done.1
  (14 shorter events, 0.1 us)
Async XLA Ops:
  8.0 85.9 %copy-start = (bf16[4096,128]{1,0:T(8,128)(2,1)S(1)}, bf16[4096,128]{1,0:T(8,128)(2,1)}, u32[]{:S(2)}) copy-start(bf16[4096,128]{1,0:T(8,128)(2,1)} %param.13) | copy-start | bytes 3145732
  8.0 89.7 %copy-start.4 = (bf16[4096,128]{1,0:T(8,128)(2,1)S(1)}, bf16[4096,128]{1,0:T(8,128)(2,1)}, u32[]{:S(2)}) copy-start(bf16[4096,128]{1,0:T(8,128)(2,1)} %param.14) | copy-start | bytes 3145732
  8.0 85.9 %all-gather.3.cloned.1.call-start = ((), (), s32[]{:S(2)}) async-start(), calls=%async_computation.1 | async-start | bytes 5242880 | tf_op jit(solution)/shard_map/all_gather | solution.py:90
  8.8 214.1 %reduce-scatter.2.cloned.1.call-start = ((), (), s32[]{:S(2)}) async-start(), calls=%async_computation.2 | async-start | bytes 11960320 | tf_op jit(solution)/shard_map/reduce_scatter | solution.py:102
  101.9 26.5 %copy-start.2 = (bf16[512,4096]{1,0:T(8,128)(2,1)S(1)}, bf16[512,4096]{1,0:T(8,128)(2,1)}, u32[]{:S(2)}) copy-start(bf16[512,4096]{1,0:T(8,128)(2,1)} %all-gather.3.cloned.1.call-done) | copy-start | bytes 12582916
  128.4 4.7 %copy-start.3 = (f32[512,4096]{0,1:T(8,128)S(1)}, f32[512,4096]{0,1:T(8,128)}, u32[]{:S(2)}) copy-start(f32[512,4096]{0,1:T(8,128)} %fusion.44) | copy-start | bytes 25165828
  142.9 0.7 copy-start.6
  142.9 0.7 copy-start.7
  142.9 1.0 copy-start.5
  142.9 131.9 %all-gather.5.cloned.1.call-start = ((), (), s32[]{:S(2)}) async-start(), calls=%async_computation.3 | async-start | bytes 6291456 | tf_op jit(solution)/shard_map/all_gather | solution.py:119
  296.8 3.5 %copy-start.1 = (bf16[4096,128]{1,0:T(8,128)(2,1)S(1)}, bf16[4096,128]{1,0:T(8,128)(2,1)}, u32[]{:S(2)}) copy-start(bf16[4096,128]{1,0:T(8,128)(2,1)} %param.13) | copy-start | bytes 3145732
Sparse Core Ops, SparseCore 0:
  10.4 83.4 all-gather.2
  143.0 79.7 reduce-scatter.1
Sparse Core Ops, SparseCore 1:
  144.9 12.6 all-gather.4
where the time goes:
time: 308 us
  waiting for transfers between devices  161 us (52%)
  blocking collectives  55.6 us (18%)
  matrix products  48 us (16%)
  other arithmetic  20.6 us (7%)
  between operations  15.8 us (5%)
  local copies, waits for them, and re-layouts  6.82 us (2%)
    all_gather x1, waiting for transfers between devices, shards(): shard_rows = lax.all_gather(tokens, 'tensor', axis=0, tiled=True)  82.9 us
    reduce_scatter x1, waiting for transfers between devices, shards(): lax.psum_scatter(partial_terms, ('seq', 'load'), scatter_dimension=0, til...  76.7 us
    dot_general x6, matrix products, product(): return jnp.dot(left, right, preferred_element_type=jnp.float32)  44.5 us
    all_gather x1, blocking collectives, shards(): kv_all = lax.all_gather(kv_local, 'tensor', axis=1, tiled=True)  15.4 us
    all_gather x1, blocking collectives, shards(): lax.all_gather(low_keyval, 'tensor', axis=1, tiled=True)  13.2 us
    all_gather x1, blocking collectives, shards(): lax.all_gather(low_query, 'tensor', axis=1, tiled=True)  13.1 us
    concatenate x1, other arithmetic, shards(): partial_terms = jnp.concatenate(columns_list, axis=1)  9.75 us
  transfers between devices with their start and end apart: 3, of which 2 were waited for; matrix products, arithmetic and copies ran while one was open for 2% of the time, Pallas kernels for 0%

commit v1 on v0

--- a/solution.py
+++ b/solution.py
@@ -1,3 +1,4 @@
+import functools
 import math
 import jax
 import jax.numpy as jnp
@@ -10,6 +11,20 @@
 TENANTS = 4
 ROPE_BASE = 500000.0
 ADAPTER_ALPHA = 8.0
+
+
+def _recover_hubs(field, dim_k):
+    world = lax.axis_size("tensor")
+    lanes = [field]
+    for hop_no in [*range(world - 1)]:
+        near = lax.ppermute(lanes[-1], "tensor", [(kk, (kk + 1) % world) for kk in range(world)])
+        lanes.append(near)
+    v1 = jnp.concatenate(lanes[::-1], axis=dim_k)
+    mixed_arr = lax.axis_index("tensor")
+    return jnp.roll(v1, (mixed_arr + 1) * field.shape[dim_k], axis=dim_k)
+
+
+store_sections_all = functools.partial(_recover_hubs, dim_k=1)
 
 
 def product(left, right):
@@ -130,7 +145,7 @@
     kv_local = jnp.where(
         is_key[None, :], rotate_pairs(keyval, position, kv_first_col), keyval
     ).astype(jnp.bfloat16)
-    kv_all = lax.all_gather(kv_local, "tensor", axis=1, tiled=True)
+    kv_all = store_sections_all(kv_local)
     heads_here = query_cols // HEAD_DIM
     group_size = HEADS // KV_HEADS
     kv_here = max(heads_here // group_size, 1)

time: 308 us -> 305 us (level)
  blocking collectives: 55.6 us -> 40.2 us
  waiting for transfers between devices: 161 us -> 166 us
  starting transfers between devices: 0.12 us -> 3.36 us
    all_gather x1 -> x0, blocking collectives: 15.4 us -> none  [shards(): kv_all = lax.all_gather(kv_local, 'tensor', axis=1, tiled=True)]
    ppermute x0 -> x3, waiting for transfers between devices: none -> 5.11 us  [_recover_hubs(): lax.ppermute(lanes[-1], 'tensor', [(kk, (kk + 1) % world) for kk in range...]
    ppermute x0 -> x3, starting transfers between devices: none -> 3.24 us  [_recover_hubs(): lax.ppermute(lanes[-1], 'tensor', [(kk, (kk + 1) % world) for kk in range...]
  transfers between devices with their start and end apart: 3 -> 6, of which waited for: 2 -> 4; matrix products, arithmetic and copies ran while one was open for 2% -> 7% of each run, Pallas kernels for 0% -> 0%
where the time goes in v1:
time: 305 us
  waiting for transfers between devices  166 us (54%)
  matrix products  48 us (16%)
  blocking collectives  40.2 us (13%)
  other arithmetic  22.5 us (7%)
  between operations  15.9 us (5%)
  local copies, waits for them, and re-layouts  8.79 us (3%)
  starting transfers between devices  3.36 us (1%)
    all_gather x1, waiting for transfers between devices, shards(): shard_rows = lax.all_gather(tokens, 'tensor', axis=0, tiled=True)  82.9 us
    reduce_scatter x1, waiting for transfers between devices, shards(): lax.psum_scatter(partial_terms, ('seq', 'load'), scatter_dimension=0, til...  76.7 us
    dot_general x6, matrix products, product(): return jnp.dot(left, right, preferred_element_type=jnp.float32)  44.5 us
    all_gather x1, blocking collectives, shards(): lax.all_gather(low_keyval, 'tensor', axis=1, tiled=True)  13.2 us
    all_gather x1, blocking collectives, shards(): lax.all_gather(low_query, 'tensor', axis=1, tiled=True)  13.1 us
    concatenate x1, other arithmetic, shards(): partial_terms = jnp.concatenate(columns_list, axis=1)  9.76 us
  transfers between devices with their start and end apart: 6, of which 4 were waited for; matrix products, arithmetic and copies ran while one was open for 7% of the time, Pallas kernels for 0%

profile of v1, /device:TPU:0, one launch (start us, length us, event | category | flops | bytes accessed | tf_op | source)
XLA Modules:
  0.0 304.7 jit_solution(8174041308665925283)
XLA Ops:
  8.0 0.0 copy-start
  8.0 0.0 copy-start.4
  8.0 0.0 all-gather.3.cloned.1.call-start
  8.1 0.7 all-gather.3.cloned.1.call-update
  8.8 0.0 reduce-scatter.2.cloned.1.call-start
  8.8 0.8 reduce-window.8
  9.6 0.7 bitcast_subtract_fusion
  10.3 0.7 select_reduce_fusion.2
  11.0 82.9 %all-gather.3.cloned.1.call-done = bf16[512,4096]{1,0:T(8,128)(2,1)} async-done(((bf16[128,4096]{1,0:T(8,128)(2,1)}), bf16[512,4096]{1,0:T(8,128)(2,1)}) %all-gather.3.cloned.1.call-update) | async-done | bytes 4194320 | tf_op jit(solution)/shard_map/all_gather | solution.py:105
  93.9 0.0 copy-done
  93.9 3.7 %fusion.46 = f32[512,128]{0,1:T(8,128)S(1)} fusion(bf16[512,4096]{1,0:T(8,128)(2,1)} %all-gather.3.cloned.1.call-done, bf16[4096,128]{1,0:T(8,128)(2,1)S(1)} %copy-done), kind=kOutput, calls=%fused_computation.108 | convolution fusion | flops 536870912 | bytes 5505024 | tf_op jit(solution)/shard_map/dot_general | solution.py:31
  97.6 0.1 reshape.386
  97.7 0.0 copy-done.4
  97.7 3.7 %fusion.47 = f32[512,128]{0,1:T(8,128)S(1)} fusion(bf16[512,4096]{1,0:T(8,128)(2,1)} %all-gather.3.cloned.1.call-done, bf16[4096,128]{1,0:T(8,128)(2,1)S(1)} %copy-done.4), kind=kOutput, calls=%fused_computation.109 | convolution fusion | flops 536870912 | bytes 5505024 | tf_op jit(solution)/shard_map/dot_general | solution.py:31
  101.4 0.1 reshape.387
  101.5 0.3 select_reduce_fusion.1
  101.9 0.0 copy-start.2
  101.9 26.5 %fusion.44 = f32[512,4096]{0,1:T(8,128)} fusion(bf16[512,4096]{1,0:T(8,128)(2,1)} %all-gather.3.cloned.1.call-done, bf16[4096,4096]{1,0:T(8,128)(2,1)} %param.11), kind=kOutput, calls=%fused_computation.106 | convolution fusion | flops 17179869184 | bytes 46137344 | tf_op jit(solution)/shard_map/dot_general | solution.py:31
  128.4 0.0 copy-done.2
  128.4 4.7 %fusion.45 = f32[512,512]{0,1:T(8,128)S(1)} fusion(bf16[512,4096]{1,0:T(8,128)(2,1)S(1)} %copy-done.2, bf16[4096,512]{1,0:T(8,128)(2,1)} %param.12), kind=kOutput, calls=%fused_computation.107 | convolution fusion | flops 2147483648 | bytes 9437184 | tf_op jit(solution)/shard_map/dot_general | solution.py:31
  133.1 9.8 %pad_maximum_fusion = f32[512,4672]{0,1:T(8,128)} fusion(f32[512,32]{0,1:T(8,128)S(1)} %get-tuple-element.13, f32[512,32]{0,1:T(8,128)S(1)} %get-tuple-element.12, f32[512,512]{0,1:T(8,128)S(1)} %fusion.45, f32[512,4096]{0,1:T(8,128)S(1)} %copy-done.3), kind=kLoop, calls=%fused_computation | loop fusion | flops 7176192 | bytes 19136512 | tf_op jit(solution)/shard_map/concatenate | solution.py:116
  142.9 0.0 reduce-scatter.2.cloned.1.call-update
  142.9 0.0 all-gather.5.cloned.1.call-start
  143.0 0.5 all-gather.5.cloned.1.call-update
  143.6 0.1 select_reduce_fusion.5
  143.7 0.1 copy-done.5
  143.9 2.2 all_gather.23
  146.0 0.1 fusion.20
  146.1 76.7 %reduce-scatter.2.cloned.1.call-done = f32[128,4672]{0,1:T(8,128)} async-done(((f32[512,4672]{0,1:T(8,128)}), f32[128,4672]{0,1:T(8,128)}) %reduce-scatter.2.cloned.1.call-update) | async-done | bytes 2392080 | tf_op jit(solution)/shard_map/reduce_scatter | solution.py:117
  222.9 0.8 fusion.27
  223.7 13.2 %all_gather.22 = bf16[128,128]{0,1:T(8,128)(2,1)S(1)} all-gather(bf16[128,32]{0,1:T(8,128)(2,1)S(1)} %get-tuple-element.17), channel_id=1, replica_groups=mesh['groups'=2,'tensor'=4,'seq'=2,'load'=2] {'tensor'}, dimensions={1}, use_global_device_ids=true | all-gather | bytes 40960 | tf_op jit(solution)/shard_map/all_gather | solution.py:129
  236.8 13.1 %all_gather.25 = bf16[128,128]{0,1:T(8,128)(2,1)S(1)} all-gather(bf16[128,32]{0,1:T(8,128)(2,1)S(1)} %get-tuple-element.18), channel_id=1, replica_groups=mesh['groups'=2,'tensor'=4,'seq'=2,'load'=2] {'tensor'}, dimensions={1}, use_global_device_ids=true | all-gather | bytes 40960 | tf_op jit(solution)/shard_map/all_gather | solution.py:128
  250.0 0.1 broadcast_select_fusion.1
  250.1 1.3 convolution_add_fusion.1
  251.4 0.2 fusion.43
  251.6 0.1 copy.76
  251.7 0.1 copy.77
  251.8 0.6 fusion.25
  252.4 0.1 copy.59
  252.5 0.1 select_convert_fusion
  252.7 1.8 collective-permute-start
  254.4 4.6 %convolution_add_fusion = f32[128,4096]{0,1:T(8,128)S(1)} fusion(bf16[128,512]{0,1:T(8,128)(2,1)S(1)} %bitcast.63, bf16[512,4096]{1,0:T(8,128)(2,1)} %all-gather.5.cloned.1.call-done, f32[128,4672]{0,1:T(8,128)} %reduce-scatter.2.cloned.1.call-done), kind=kOutput, calls=%fused_computation.6 | convolution fusion | flops 537395200 | bytes 8519680 | tf_op jit(solution)/shard_map/dot_general | solution.py:31
  259.1 1.7 fusion.42
  260.7 0.7 copy.78
  261.4 0.7 copy.79
  262.1 0.0 collective-permute-done
  262.1 0.1 collective-permute-start.1
  262.2 4.9 %fusion.14 = (bf16[128,2048,1]{1,0,2:T(8,128)(2,1)}, bf16[128,2048,1]{1,0,2:T(8,128)(2,1)}) fusion(f32[128,2048,1]{1,0,2:T(8,128)S(1)} %copy.79, f32[128,2048,1]{1,0,2:T(8,128)S(1)} %copy.78, f32[2048]{0:T(1024)S(1)} %fusion.35, f32[128]{0:T(128)S(1)} %subtract_convert_fusion), kind=kLoop, calls=%fused_computation.19 | loop fusion | flops 2359296 | bytes 3154432 | tf_op jit(solution)/shard_map/convert
  267.1 0.8 copy.68
  267.8 1.6 collective-permute-done.1
  269.4 1.4 collective-permute-start.2
  270.8 1.3 pad_maximum_fusion.1
  272.1 0.8 copy.64
  272.9 3.5 %collective-permute-done.2 = bf16[128,512]{0,1:T(8,128)(2,1)S(1)} collective-permute-done((bf16[128,512]{0,1:T(8,128)(2,1)}, bf16[128,512]{0,1:T(8,128)(2,1)S(1)}, u32[]{:S(2)}, u32[]{:S(2)}) %collective-permute-start.2) | collective-permute-done | bytes 131104 | tf_op jit(solution)/shard_map/ppermute | solution.py:20
  276.4 0.9 constant_dynamic-update-slice_fusion.6
  277.4 0.9 constant_dynamic-update-slice_fusion.2
  278.5 0.1 copy.60
  278.6 5.8 %all_gather.24 = bf16[512,2,128]{2,0,1:T(8,128)(2,1)S(1)} all-gather(bf16[128,2,128]{2,0,1:T(8,128)(2,1)S(1)} %copy.60), channel_id=1, replica_groups=mesh['groups'=2,'tensor'=4,'seq'=2,'load'=2] {'seq','load'}, dimensions={0}, use_global_device_ids=true | all-gather | bytes 327680 | tf_op jit(solution)/shard_map/all_gather | solution.py:163
  284.4 1.3 fusion
  285.7 5.9 %all_gather.27 = bf16[512,2,128]{0,2,1:T(8,128)(2,1)S(1)} all-gather(bf16[128,2,128]{0,2,1:T(8,128)(2,1)S(1)} %bitcast.66), channel_id=1, replica_groups=mesh['groups'=2,'tensor'=4,'seq'=2,'load'=2] {'seq','load'}, dimensions={0}, use_global_device_ids=true | all-gather | bytes 327680 | tf_op jit(solution)/shard_map/all_gather | solution.py:164
  291.6 2.0 fusion.1
  293.7 0.0 copy-start.1
  293.7 2.2 fusion.6
  295.9 1.3 copy.67
  (27 shorter events, 0.3 us)
Async XLA Ops:
  8.0 85.9 %copy-start = (bf16[4096,128]{1,0:T(8,128)(2,1)S(1)}, bf16[4096,128]{1,0:T(8,128)(2,1)}, u32[]{:S(2)}) copy-start(bf16[4096,128]{1,0:T(8,128)(2,1)} %param.13) | copy-start | bytes 3145732
  8.0 89.7 %copy-start.4 = (bf16[4096,128]{1,0:T(8,128)(2,1)S(1)}, bf16[4096,128]{1,0:T(8,128)(2,1)}, u32[]{:S(2)}) copy-start(bf16[4096,128]{1,0:T(8,128)(2,1)} %param.14) | copy-start | bytes 3145732
  8.0 85.9 %all-gather.3.cloned.1.call-start = ((), (), s32[]{:S(2)}) async-start(), calls=%async_computation.1 | async-start | bytes 5242880 | tf_op jit(solution)/shard_map/all_gather | solution.py:105
  8.8 214.1 %reduce-scatter.2.cloned.1.call-start = ((), (), s32[]{:S(2)}) async-start(), calls=%async_computation.2 | async-start | bytes 11960320 | tf_op jit(solution)/shard_map/reduce_scatter | solution.py:117
  101.9 26.5 %copy-start.2 = (bf16[512,4096]{1,0:T(8,128)(2,1)S(1)}, bf16[512,4096]{1,0:T(8,128)(2,1)}, u32[]{:S(2)}) copy-start(bf16[512,4096]{1,0:T(8,128)(2,1)} %all-gather.3.cloned.1.call-done) | copy-start | bytes 12582916
  128.4 4.7 %copy-start.3 = (f32[512,4096]{0,1:T(8,128)S(1)}, f32[512,4096]{0,1:T(8,128)}, u32[]{:S(2)}) copy-start(f32[512,4096]{0,1:T(8,128)} %fusion.44) | copy-start | bytes 25165828
  142.9 0.8 copy-start.6
  142.9 0.8 copy-start.7
  142.9 1.0 copy-start.5
  142.9 111.5 %all-gather.5.cloned.1.call-start = ((), (), s32[]{:S(2)}) async-start(), calls=%async_computation.3 | async-start | bytes 6291456 | tf_op jit(solution)/shard_map/all_gather | solution.py:134
  252.7 9.4 %collective-permute-start = (bf16[128,512]{0,1:T(8,128)(2,1)S(1)}, bf16[128,512]{0,1:T(8,128)(2,1)S(1)}, u32[]{:S(2)}, u32[]{:S(2)}) collective-permute-start(bf16[128,512]{0,1:T(8,128)(2,1)S(1)} %select_convert_fusion), channel_id=1, source_target_pairs={{0,4},{4,8},{8,12},{12,0},{1,5},{5,9},{9,13},{13,1},{2,6},{6,10},{... | collective-permute-start | bytes 393224 | tf_op jit(solution)/shard_map/ppermute | solution.py:20
  262.1 7.4 %collective-permute-start.1 = (bf16[128,512]{0,1:T(8,128)(2,1)S(1)}, bf16[128,512]{0,1:T(8,128)(2,1)}, u32[]{:S(2)}, u32[]{:S(2)}) collective-permute-start(bf16[128,512]{0,1:T(8,128)(2,1)S(1)} %collective-permute-done), channel_id=1, source_target_pairs={{0,4},{4,8},{8,12},{12,0},{1,5},{5,9},{9,13},{13,1},{2,6},{6,10},{... | collective-permute-start | bytes 393224 | tf_op jit(solution)/shard_map/ppermute | solution.py:20
  269.4 7.0 %collective-permute-start.2 = (bf16[128,512]{0,1:T(8,128)(2,1)}, bf16[128,512]{0,1:T(8,128)(2,1)S(1)}, u32[]{:S(2)}, u32[]{:S(2)}) collective-permute-start(bf16[128,512]{0,1:T(8,128)(2,1)} %collective-permute-done.1), channel_id=1, source_target_pairs={{0,4},{4,8},{8,12},{12,0},{1,5},{5,9},{9,13},{13,1},{2,6},{6,10},{... | collective-permute-start | bytes 393224 | tf_op jit(solution)/shard_map/ppermute | solution.py:20
  293.7 3.5 %copy-start.1 = (bf16[4096,128]{1,0:T(8,128)(2,1)S(1)}, bf16[4096,128]{1,0:T(8,128)(2,1)}, u32[]{:S(2)}) copy-start(bf16[4096,128]{1,0:T(8,128)(2,1)} %param.13) | copy-start | bytes 3145732
Sparse Core Ops, SparseCore 0:
  10.4 83.4 all-gather.2
  143.0 79.7 reduce-scatter.1
Sparse Core Ops, SparseCore 1:
  144.9 12.6 all-gather.4
